TPU v7x, 32 devices: a whole 2x2x4 slice. The times are simulated.
32 devices in a mesh: lang: 4 (over x, core), dp: 8 (over z, y).
Axes of the slice: x: 2, y: 2, z: 4, core: 2. Of those that a mesh axis runs over, the one named last changes fastest.
Arguments:
- src_emb: bfloat16 [4096, 768], P(('lang', 'dp')), may hold values from -6 to 6
- tgt_emb: bfloat16 [4, 1024, 768], P(None, ('lang', 'dp')), may hold values from -6 to 6
- slot_group: int32 [4], replicated, may hold values from 0 to 3, each once
- counts: int32 [4], replicated, may hold values from 256 to 1024, as said below
- align: int32 [4, 1024], P('lang'), may hold values from 0 to 1023, each once within a row
- pair_weight: float32 [4], replicated, may hold values from 4 to 40
Outputs:
- grad_src: bfloat16 [4096, 768], P(('lang', 'dp'))
- grad_tgt: bfloat16 [4, 1024, 768], P(None, ('lang', 'dp'))
- pair_loss: float32 [4], P('lang')
Inputs may be any that keep to these rules, and one draw needn't show every extreme that they name: `counts`: at least one pair has all 1024 sentences live. `align`: each row is a permutation.
All inputs are finite; a program needn't handle non-finite values.
Results may differ from a plain program's by a relative error of at most 0.0057.
Values may be sent and summed in bfloat16 or wider, within the bound.
No kernel may reach another device: no remote copies, remote signals or barrier semaphores. Data moves between devices by JAX's collectives and lax.ppermute only.
A program may use at most 64 MiB of HBM per device.

v0:
```python
import math
import jax
import jax.numpy as jnp
from jax import lax
from jax.sharding import PartitionSpec as P

MARGIN = 0.3
LOW_FILL = -1e30
BLOCK_BYTES = 8 * 1024 * 1024


def target_index(col_count, row_count, per_slot, data_size):
    position = jnp.arange(col_count, dtype=jnp.int32)
    source = position // row_count
    within = position % row_count
    return (within // per_slot * data_size + source) * per_slot + within % per_slot


def scores_of(x_rows, y_rows, pos_mask, inv_root):
    raw_dot = lax.dot_general(
        x_rows, y_rows, (((1,), (1,)), ((), ())), preferred_element_type=jnp.float32
    )
    return raw_dot * inv_root - MARGIN * pos_mask.astype(jnp.float32)


def block_stats(scores_f, is_pos, row_live, col_ok):
    row_max = jnp.max(jnp.where(col_ok[None, :], scores_f, LOW_FILL), axis=1)
    row_sum = jnp.sum(jnp.where(col_ok[None, :], jnp.exp(scores_f - row_max[:, None]), 0.0), axis=1)
    row_lse = row_max + jnp.log(row_sum + (1.0 - row_live.astype(jnp.float32)))
    pos_score = jnp.sum(jnp.where(is_pos, scores_f, 0.0), axis=1)
    col_max = jnp.max(jnp.where(row_live[:, None], scores_f, LOW_FILL), axis=0)
    col_sum = jnp.sum(
        jnp.where(row_live[:, None], jnp.exp(scores_f - col_max[None, :]), 0.0), axis=0
    )
    return (row_lse, pos_score, col_max, col_sum)


def grad_of(scores_f, is_pos, row_ok, col_ok, row_lse, col_lse, weight):
    both_live = row_ok[:, None] & col_ok[None, :]
    by_row = jnp.where(both_live, jnp.exp(scores_f - row_lse[:, None]), 0.0)
    by_col = jnp.where(both_live, jnp.exp(scores_f - col_lse[None, :]), 0.0)
    pos_hit = (is_pos & row_ok[:, None]).astype(jnp.float32)
    return (weight * (by_row + by_col - 2.0 * pos_hit)).astype(jnp.bfloat16)


def per_device(src_emb, tgt_emb, slot_group, counts, align, pair_weight):
    lang_size = lax.axis_size("lang")
    data_size = lax.axis_size("dp")
    row_count, emb_width = src_emb.shape
    per_slot = tgt_emb.shape[1]
    pair_rows = row_count * data_size
    inv_root = 1.0 / math.sqrt(emb_width)
    group_index = lax.axis_index("lang")
    shard_index = lax.axis_index("dp")
    slot_ids = jnp.arange(lang_size, dtype=jnp.int32)
    slot_of_group = jnp.zeros((lang_size,), jnp.int32).at[slot_group].set(slot_ids)
    ordered = tgt_emb[slot_of_group]
    arrived = lax.all_to_all(ordered, "lang", split_axis=0, concat_axis=1, tiled=True)
    partner = arrived[0]
    live_count = counts[group_index]
    weight = pair_weight[group_index]
    pair_align = align[0]
    all_rows = jnp.arange(pair_rows, dtype=jnp.int32)
    row_live = all_rows < live_count
    col_live_global = (
        jnp.zeros((pair_rows,), jnp.int32).at[pair_align].set(row_live.astype(jnp.int32))
    )
    perm = target_index(pair_rows, row_count, per_slot, data_size)
    col_live = col_live_global[perm] > 0
    x_all = lax.all_gather(src_emb, "dp", axis=0, tiled=True)
    y_all = lax.all_gather(partner, "dp", axis=0, tiled=True)
    block = max(1, min(pair_rows, BLOCK_BYTES // (4 * pair_rows)))
    steps = pair_rows // block
    if steps == 1:
        is_pos = perm[None, :] == pair_align[:, None]
        scores_f = scores_of(x_all, y_all, is_pos, inv_root)
        row_lse, pos_score, col_max, col_sum = block_stats(scores_f, is_pos, row_live, col_live)
    else:

        def one_block(k, carry):
            row_lse, pos_score, col_max, col_sum = carry
            start = k * block
            x_blk = lax.dynamic_slice_in_dim(x_all, start, block)
            a_blk = lax.dynamic_slice_in_dim(pair_align, start, block)
            r_blk = lax.dynamic_slice_in_dim(row_live, start, block)
            is_pos = perm[None, :] == a_blk[:, None]
            s_blk = scores_of(x_blk, y_all, is_pos, inv_root)
            b_lse, b_pos, b_max, b_sum = block_stats(s_blk, is_pos, r_blk, col_live)
            top = jnp.maximum(col_max, b_max)
            col_sum = col_sum * jnp.exp(col_max - top) + b_sum * jnp.exp(b_max - top)
            row_lse = lax.dynamic_update_slice_in_dim(row_lse, b_lse, start, 0)
            pos_score = lax.dynamic_update_slice_in_dim(pos_score, b_pos, start, 0)
            return (row_lse, pos_score, top, col_sum)

        zeros = jnp.zeros((pair_rows,), jnp.float32)
        init = (zeros, zeros, jnp.full((pair_rows,), LOW_FILL, jnp.float32), zeros)
        row_lse, pos_score, col_max, col_sum = lax.fori_loop(0, steps, one_block, init)
    col_lse = col_max + jnp.log(col_sum + (1.0 - col_live.astype(jnp.float32)))
    row_f = row_live.astype(jnp.float32)
    col_f = col_live.astype(jnp.float32)
    total = jnp.sum(row_f * (row_lse - 2.0 * pos_score)) + jnp.sum(col_f * col_lse)
    pair_loss = (total / live_count.astype(jnp.float32)).reshape(1)
    mine = shard_index * row_count
    x_my = lax.dynamic_slice_in_dim(x_all, mine, row_count)
    a_my = lax.dynamic_slice_in_dim(pair_align, mine, row_count)
    r_my = lax.dynamic_slice_in_dim(row_live, mine, row_count)
    lse_my = lax.dynamic_slice_in_dim(row_lse, mine, row_count)
    pos_rows = perm[None, :] == a_my[:, None]
    s_rows = scores_of(x_my, y_all, pos_rows, inv_root)
    g_rows = grad_of(s_rows, pos_rows, r_my, col_live, lse_my, col_lse, weight)
    grad_src = (jnp.dot(g_rows, y_all, preferred_element_type=jnp.float32) * inv_root).astype(
        jnp.bfloat16
    )
    p_my = lax.dynamic_slice_in_dim(perm, mine, row_count)
    c_my = lax.dynamic_slice_in_dim(col_live, mine, row_count)
    clse_my = lax.dynamic_slice_in_dim(col_lse, mine, row_count)
    pos_cols = p_my[None, :] == pair_align[:, None]
    s_cols = scores_of(x_all, partner, pos_cols, inv_root)
    g_cols = grad_of(s_cols, pos_cols, row_live, c_my, row_lse, clse_my, weight)
    own_terms = lax.dot_general(
        g_cols, x_all, (((0,), (0,)), ((), ())), preferred_element_type=jnp.float32
    )
    grad_local = (own_terms * inv_root).astype(jnp.bfloat16)
    returned = lax.all_to_all(
        grad_local.reshape(1, row_count, emb_width), "lang", split_axis=1, concat_axis=0, tiled=True
    )
    grad_tgt = returned[slot_group]
    return (grad_src, grad_tgt, pair_loss)


def solution(mesh):
    in_specs = (
        P(("lang", "dp"), None),
        P(None, ("lang", "dp"), None),
        P(),
        P(),
        P("lang", None),
        P(),
    )
    out_specs = (P(("lang", "dp"), None), P(None, ("lang", "dp"), None), P("lang"))
    return jax.shard_map(
        per_device, mesh=mesh, in_specs=in_specs, out_specs=out_specs, check_vma=False
    )
```

profile of v0, /device:TPU:0, one launch (start us, length us, event | category | flops | bytes accessed | tf_op | source)
XLA Modules:
  0.0 133.8 jit_solution(15715575883117667560)
XLA Ops:
  7.2 0.7 all-gather.3.cloned.1.call-update
  8.0 0.7 compare_select_fusion.10
  8.6 0.6 scatter_custom_fusion.1
  9.3 0.6 gather_fusion.1
  9.8 9.4 %all_to_all.21 = bf16[4,32,768]{2,1,0:T(8,128)(2,1)} all-to-all(bf16[4,32,768]{2,1,0:T(8,128)(2,1)S(1)} %gather_fusion.1), channel_id=1, replica_groups=mesh['lang'=4,'dp'=8] {'lang'}, dimensions={0} | all-to-all | bytes 393216 | tf_op jit(solution)/shard_map/all_to_all | solution.py:58
  19.3 1.2 dynamic_slice.28
  21.2 0.7 fusion.61
  21.9 0.7 compare_select_fusion.5
  22.6 4.3 %scatter_custom_fusion = s32[1024]{0:T(1024)S(1)} fusion(s32[1024]{0:T(1024)S(1)} %bitcast.44, s32[1024]{0:T(1024)S(1)} %fusion.61, s32[]{:T(128)} %constant.94.clone.1), kind=kCustom, calls=%fused_computation.116 | custom fusion | bytes 4100 | tf_op jit(solution)/shard_map/scatter | solution.py:66
  26.9 4.5 %gather_fusion = s32[1024]{0:T(1024)S(1)} fusion(s32[1024]{0:T(1024)S(1)} %scatter_custom_fusion, s32[1024]{0:T(1024)S(1)} %broadcast_clamp_fusion), kind=kCustom, calls=%fused_computation | custom fusion | bytes 12288 | tf_op jit(solution)/shard_map/gather | solution.py:69
  31.7 0.6 dynamic_slice.27
  32.3 0.6 iota_compare_fusion
  33.0 24.2 %all-gather.3.cloned.1.call-done = bf16[1024,768]{1,0:T(8,128)(2,1)} async-done(((bf16[128,768]{1,0:T(8,128)(2,1)}), bf16[1024,768]{1,0:T(8,128)(2,1)}) %all-gather.3.cloned.1.call-update) | async-done | bytes 1572880 | tf_op jit(solution)/shard_map/all_gather | solution.py:70
  57.2 44.8 %all-gather.5.cloned.1.call-done = bf16[1024,768]{1,0:T(8,128)(2,1)} async-done(((bf16[128,768]{1,0:T(8,128)(2,1)}), bf16[1024,768]{1,0:T(8,128)(2,1)}) %all-gather.5.cloned.1.call-update) | async-done | bytes 1572880 | tf_op jit(solution)/shard_map/all_gather | solution.py:71
  101.9 4.5 %select_reduce_fusion.3 = (f32[1024]{0:T(1024)S(1)}, f32[1024]{0:T(1024)S(1)}, f32[1024,1024]{0,1:T(8,128)S(1)}) fusion(pred[1024]{0:T(1024)(128)(4,1)S(1)} %broadcast_compare_fusion, pred[1024]{0:T(1024)(128)(4,1)S(1)} %iota_compare_fusion, s32[1024]{0:T(1024)S(1)} %bitcast.40, s32[1024]{0:T(1024)S(1)} %fusion.50, ...), kind=kOutput, calls=%fused_computation.12 | convolution fusion | flops 1618999296 | bytes 7358464 | tf_op jit(solution)/shard_map/dot_general | solution.py:20
  106.5 2.5 %fusion.1 = (f32[1024]{0:T(1024)S(1)}, f32[1024]{0:T(1024)S(1)}, f32[1024]{0:T(1024)S(1)}) fusion(f32[1024,1024]{0,1:T(8,128)S(1)} %get-tuple-element.12, s32[1024]{0:T(1024)S(1)} %bitcast.41, s32[1024]{0:T(1024)S(1)} %fusion.50, f32[1024]{0:T(1024)S(1)} %get-tuple-element.7, pred[1024]{0:T(1024)(128)(4,1)S(1)} %iota_compare_fusion, ...), kind=kLoop, calls=%fused_computation.8 | loop fusion | flops 9434112 | bytes 4225024 | tf_op jit(solution)/shard_map/reduce_sum | solution.py:30
  108.9 1.3 select_reduce_fusion.4
  110.4 1.7 %fusion.7 = bf16[1,128,768]{2,1,0:T(8,128)(2,1)S(1)} fusion(bf16[1024,768]{1,0:T(8,128)(2,1)S(1)} %copy-done.3, bf16[128,768]{1,0:T(8,128)(2,1)S(1)} %bitcast.38, f32[128]{0:T(128)S(1)} %dynamic_slice.35, f32[1024]{0:T(1024)S(1)} %get-tuple-element.14, s32[1024]{0:T(1024)S(1)} %bitcast.42, f32[]{:T(128)} %bitcast, s32[128]{0:T(128)S(1)} %dynamic_slice.34, ...), kind=kOutput, calls=%fused_computation.22 | convolution fusion | flops 404815872 | bytes 1976452 | tf_op jit(solution)/shard_map/dot_general | solution.py:120
  112.4 0.5 broadcast.415
  112.9 1.8 %reduce = bf16[128,768]{1,0:T(8,128)(2,1)S(1)} reduce(bf16[128,1,768]{2,1,0:T(2,128)(2,1)S(1)} %bitcast.36, bf16[]{:T(256)} %broadcast.415), dimensions={1}, to_apply=%bitcast.34.reduce_sub_computation | reduce | bytes 393218
  114.7 0.7 reshape.320
  115.5 3.4 %all-to-all-start.1 = ((bf16[4,2,12288]{2,1,0:T(2,128)(2,1)}), bf16[4,2,12288]{2,1,0:T(2,128)(2,1)S(1)}, u32[]{:S(2)}, u32[]{:S(2)}) async-start(bf16[4,2,12288]{2,1,0:T(2,128)(2,1)} %reshape.320), calls=%async_computation.1 | async-start | bytes 393216 | tf_op jit(solution)/shard_map/all_to_all | solution.py:124
  118.8 4.2 %fusion.5 = bf16[128,768]{1,0:T(8,128)(2,1)} fusion(bf16[1024,768]{1,0:T(8,128)(2,1)} %all-gather.5.cloned.1.call-done, f32[1024]{0:T(1024)S(1)} %get-tuple-element.9, f32[128]{0:T(128)S(1)} %dynamic_slice.32, s32[1024]{0:T(1024)S(1)} %fusion.50, f32[]{:T(128)} %bitcast, s32[128]{0:T(128)S(1)} %dynamic-slice_bitcast_fusion, ...), kind=kOutput, calls=%fused_computation.20 | convolution fusion | flops 404815872 | bytes 3550212 | tf_op jit(solution)/shard_map/dot_general | solution.py:111
  124.6 1.2 gather_fusion.2
  (31 shorter events, 1.1 us)
Async XLA Ops:
  7.2 2.1 %copy-start = (bf16[4,32,768]{2,1,0:T(8,128)(2,1)S(1)}, bf16[4,32,768]{2,1,0:T(8,128)(2,1)}, u32[]{:S(2)}) copy-start(bf16[4,32,768]{2,1,0:T(8,128)(2,1)} %param.7) | copy-start | bytes 589828
  7.2 25.8 %copy-start.2 = (s32[1,1024]{1,0:T(1,128)S(1)}, s32[1,1024]{1,0:T(1,128)}, u32[]{:S(2)}) copy-start(s32[1,1024]{1,0:T(1,128)} %param.10) | copy-start | bytes 12292
  7.2 24.5 %copy-start.4 = (f32[4]{0:T(128)S(1)}, f32[4]{0:T(128)}, u32[]{:S(2)}) copy-start(f32[4]{0:T(128)} %param.11) | copy-start | bytes 52
  7.2 50.0 %all-gather.3.cloned.1.call-start = ((), (), s32[]{:S(2)}) async-start(), calls=%async_computation.2 | async-start | bytes 1769472 | tf_op jit(solution)/shard_map/all_gather | solution.py:70
  7.9 94.0 %all-gather.5.cloned.1.call-start = ((), (), s32[]{:S(2)}) async-start(), calls=%async_computation.3 | async-start | bytes 1769472 | tf_op jit(solution)/shard_map/all_gather | solution.py:71
  106.4 4.0 %copy-start.1 = (bf16[4,32,768]{2,1,0:T(8,128)(2,1)S(1)}, bf16[4,32,768]{2,1,0:T(8,128)(2,1)}, u32[]{:S(2)}) copy-start(bf16[4,32,768]{2,1,0:T(8,128)(2,1)} %all_to_all.21) | copy-start | bytes 589828
  106.4 3.9 %copy-start.3 = (bf16[1024,768]{1,0:T(8,128)(2,1)S(1)}, bf16[1024,768]{1,0:T(8,128)(2,1)}, u32[]{:S(2)}) copy-start(bf16[1024,768]{1,0:T(8,128)(2,1)} %all-gather.3.cloned.1.call-done) | copy-start | bytes 4718596
  115.5 8.9 %all-to-all-start.1 = ((bf16[4,2,12288]{2,1,0:T(2,128)(2,1)}), bf16[4,2,12288]{2,1,0:T(2,128)(2,1)S(1)}, u32[]{:S(2)}, u32[]{:S(2)}) async-start(bf16[4,2,12288]{2,1,0:T(2,128)(2,1)} %reshape.320), calls=%async_computation.1 | async-start | bytes 393216 | tf_op jit(solution)/shard_map/all_to_all | solution.py:124
Sparse Core Ops, SparseCore 0:
  10.2 46.9 all-gather.2
  59.4 42.5 all-gather.4
where the time goes:
time: 134 us
  waiting for transfers between devices  69.6 us (52%)
  between operations  17.3 us (13%)
  local copies, waits for them, and re-layouts  15.2 us (11%)
  matrix products  10.4 us (8%)
  blocking collectives  9.44 us (7%)
  other arithmetic  8.34 us (6%)
  starting transfers between devices  3.44 us (3%)
    all_gather x1, waiting for transfers between devices, per_device(): y_all = lax.all_gather(partner, 'dp', axis=0, tiled=True)  44.8 us
    all_gather x1, waiting for transfers between devices, per_device(): x_all = lax.all_gather(src_emb, 'dp', axis=0, tiled=True)  24.2 us
    all_to_all x1, blocking collectives, per_device(): lax.all_to_all(ordered, 'lang', split_axis=0, concat_axis=1, tiled=True)  9.44 us
    gather x1, local copies, waits for them, and re-layouts, per_device(): col_live = col_live_global[perm] > 0  4.53 us
    dot_general x1, matrix products, scores_of(): lax.dot_general(x_rows, y_rows, (((1,), (1,)), ((), ())), preferred_eleme...  4.5 us
    scatter x1, local copies, waits for them, and re-layouts, per_device(): jnp.zeros((pair_rows,), jnp.int32).at[pair_align]  4.31 us
    dot_general x1, matrix products, per_device(): jnp.dot(g_rows, y_all, preferred_element_type=jnp.float32) * inv_root  4.24 us
    all_to_all x1, starting transfers between devices, per_device(): lax.all_to_all(grad_local.reshape(1, row_count, emb_width), 'lang', split...  3.37 us
  transfers between devices with their start and end apart: 3, of which 2 were waited for; matrix products, arithmetic and copies ran while one was open for 14% of the time, Pallas kernels for 0%

commit v1 on v0

--- a/solution.py
+++ b/solution.py
@@ -67,8 +67,11 @@
     )
     perm = target_index(pair_rows, row_count, per_slot, data_size)
     col_live = col_live_global[perm] > 0
-    x_all = lax.all_gather(src_emb, "dp", axis=0, tiled=True)
-    y_all = lax.all_gather(partner, "dp", axis=0, tiled=True)
+    x_all, y_all = jnp.split(
+        lax.all_gather(jnp.concatenate([src_emb, partner], axis=1), "dp", axis=0, tiled=True),
+        [src_emb.shape[1]],
+        axis=1,
+    )
     block = max(1, min(pair_rows, BLOCK_BYTES // (4 * pair_rows)))
     steps = pair_rows // block
     if steps == 1:

time: 134 us -> 119 us (0.89)
  waiting for transfers between devices: 69.6 us -> 44.7 us
  local copies, waits for them, and re-layouts: 15.2 us -> 20.9 us
  other arithmetic: 8.34 us -> 10.9 us
    all_gather x2 -> x1, waiting for transfers between devices: 68.9 us -> 44.7 us  [per_device(): lax.all_gather(jnp.concatenate([src_emb, partner], axis=1), 'dp', axis=0,...]
    concatenate x0 -> x1, other arithmetic: none -> 1.7 us  [per_device(): jnp.concatenate([src_emb, partner], axis=1)]
    split x0 -> x1, local copies, waits for them, and re-layouts: none -> 1.51 us  [per_device(): jnp.split(lax.all_gather(jnp.concatenate([src_emb, partner], axis=1), 'dp...]
    dot_general x1, matrix products: 1.68 us -> 3.12 us  [per_device(): lax.dot_general(g_cols, x_all, (((0,), (0,)), ((), ())), preferred_elemen...]
  transfers between devices with their start and end apart: 3 -> 2, of which waited for: 2 -> 1; matrix products, arithmetic and copies ran while one was open for 14% -> 18% of each run, Pallas kernels for 0% -> 0%
where the time goes in v1:
time: 119 us; the launch traced here: 118 us
  waiting for transfers between devices  44.7 us (38%)
  local copies, waits for them, and re-layouts  20.9 us (18%)
  between operations  17.4 us (15%)
  matrix products  11.6 us (10%)
  other arithmetic  10.9 us (9%)
  blocking collectives  9.34 us (8%)
  starting transfers between devices  3.4 us (3%)
    all_gather x1, waiting for transfers between devices, per_device(): lax.all_gather(jnp.concatenate([src_emb, partner], axis=1), 'dp', axis=0,...  44.7 us
    all_to_all x1, blocking collectives, per_device(): lax.all_to_all(ordered, 'lang', split_axis=0, concat_axis=1, tiled=True)  9.34 us
    gather x1, local copies, waits for them, and re-layouts, per_device(): col_live = col_live_global[perm] > 0  4.53 us
    scatter x1, local copies, waits for them, and re-layouts, per_device(): jnp.zeros((pair_rows,), jnp.int32).at[pair_align]  4.31 us
    dot_general x1, matrix products, scores_of(): lax.dot_general(x_rows, y_rows, (((1,), (1,)), ((), ())), preferred_eleme...  4.25 us
    dot_general x1, matrix products, per_device(): jnp.dot(g_rows, y_all, preferred_element_type=jnp.float32) * inv_root  4.24 us
    all_to_all x1, starting transfers between devices, per_device(): lax.all_to_all(grad_local.reshape(1, row_count, emb_width), 'lang', split...  3.37 us
    reduce_sum x1, other arithmetic, block_stats(): pos_score = jnp.sum(jnp.where(is_pos, scores_f, 0.0), axis=1)  3.28 us
  transfers between devices with their start and end apart: 2, of which 1 were waited for; matrix products, arithmetic and copies ran while one was open for 18% of the time, Pallas kernels for 0%

profile of v1, /device:TPU:0, one launch (start us, length us, event | category | flops | bytes accessed | tf_op | source)
XLA Modules:
  0.0 118.3 jit_solution(16725916422620188701)
XLA Ops:
  7.2 0.7 compare_select_fusion.10
  9.2 9.3 %all_to_all.21 = bf16[4,32,768]{2,1,0:T(8,128)(2,1)S(1)} all-to-all(bf16[4,32,768]{2,1,0:T(8,128)(2,1)S(1)} %gather_fusion.1), channel_id=1, replica_groups=mesh['lang'=4,'dp'=8] {'lang'}, dimensions={0} | all-to-all | bytes 393216 | tf_op jit(solution)/shard_map/all_to_all | solution.py:58
  18.5 1.7 %pad_maximum_fusion = bf16[128,1536]{1,0:T(8,128)(2,1)} fusion(bf16[128,768]{1,0:T(8,128)(2,1)S(1)} %bitcast.21, bf16[128,768]{1,0:T(8,128)(2,1)} %param.6), kind=kLoop, calls=%fused_computation.41 | loop fusion | flops 786432 | bytes 786432 | tf_op jit(solution)/shard_map/concatenate | solution.py:71
  20.2 1.2 %dynamic_slice.28 = s32[1]{0:T(128)} dynamic-slice(s32[4]{0:T(128)} %param.9, s32[]{:T(128)S(6)} %select_n.159), dynamic_slice_sizes={1} | dynamic-slice | bytes 12 | tf_op jit(solution)/shard_map/dynamic_slice | solution.py:60
  22.1 0.6 fusion.69
  22.8 0.7 compare_select_fusion.5
  23.5 4.3 %scatter_custom_fusion = s32[1024]{0:T(1024)S(1)} fusion(s32[1024]{0:T(1024)S(1)} %bitcast.28, s32[1024]{0:T(1024)S(1)} %fusion.69, s32[]{:T(128)} %constant.94.clone.1), kind=kCustom, calls=%fused_computation.119 | custom fusion | bytes 4100 | tf_op jit(solution)/shard_map/scatter | solution.py:66
  27.8 4.5 %gather_fusion = s32[1024]{0:T(1024)S(1)} fusion(s32[1024]{0:T(1024)S(1)} %scatter_custom_fusion, s32[1024]{0:T(1024)S(1)} %broadcast_clamp_fusion), kind=kCustom, calls=%fused_computation | custom fusion | bytes 12288 | tf_op jit(solution)/shard_map/gather | solution.py:69
  32.4 0.6 dynamic_slice.33
  33.0 0.6 dynamic_slice.34
  34.2 0.6 iota_compare_fusion
  34.9 0.6 dynamic_slice.29
  36.0 44.7 %all-gather.2.cloned.1.call-done = bf16[1024,1536]{1,0:T(8,128)(2,1)} async-done(((bf16[128,1536]{1,0:T(8,128)(2,1)}), bf16[1024,1536]{1,0:T(8,128)(2,1)}) %all-gather.2.cloned.1.call-update) | async-done | bytes 3145744 | tf_op jit(solution)/shard_map/all_gather | solution.py:71
  80.7 4.3 %select_reduce_fusion.3 = (f32[1024]{0:T(1024)S(1)}, f32[1024]{0:T(1024)S(1)}, f32[1024,1024]{0,1:T(8,128)S(1)}) fusion(pred[1024]{0:T(1024)(128)(4,1)S(1)} %broadcast_compare_fusion, pred[1024]{0:T(1024)(128)(4,1)S(1)} %iota_compare_fusion, s32[1024]{0:T(1024)S(1)} %bitcast.24, s32[1024]{0:T(1024)S(1)} %fusion.58, ...), kind=kOutput, calls=%fused_computation.12 | convolution fusion | flops 1618999296 | bytes 7358464 | tf_op jit(solution)/shard_map/dot_general | solution.py:20
  85.0 3.3 %fusion.1 = (f32[1024]{0:T(1024)S(1)}, f32[1024]{0:T(1024)S(1)}, f32[1024]{0:T(1024)S(1)}) fusion(f32[1024,1024]{0,1:T(8,128)S(1)} %get-tuple-element.12, s32[1024]{0:T(1024)S(1)} %bitcast.25, s32[1024]{0:T(1024)S(1)} %fusion.58, f32[1024]{0:T(1024)S(1)} %get-tuple-element.7, pred[1024]{0:T(1024)(128)(4,1)} %copy-done.8, f32[1024]{0:T(1024)S(1)} %get-tuple-element.6, ...), kind=kLoop, calls=%fused_computation.8 | loop fusion | flops 9434112 | bytes 4225024 | tf_op jit(solution)/shard_map/reduce_sum | solution.py:30
  88.3 1.3 %select_reduce_fusion.4 = (f32[]{:T(128)}, f32[1024]{0:T(1024)S(1)}, f32[]{:T(128)}, f32[1024]{0:T(1024)S(1)}) fusion(f32[1024]{0:T(1024)S(1)} %get-tuple-element.7, f32[1024]{0:T(1024)S(1)} %get-tuple-element.4, f32[1024]{0:T(1024)S(1)} %get-tuple-element.3, f32[1024]{0:T(1024)S(1)} %get-tuple-element.6, f32[1024]{0:T(1024)S(1)} %get-tuple-element.5, ...), kind=kLoop, calls=%fused_computation.105 | loop fusion | flops 16382 | bytes 32780 | tf_op jit(solution)/shard_map/reduce_sum | solution.py:104
  90.9 3.1 %fusion.11 = bf16[1,128,768]{2,1,0:T(8,128)(2,1)} fusion(bf16[128,768]{1,0:T(8,128)(2,1)S(1)} %bitcast.22, f32[128]{0:T(128)S(1)} %dynamic_slice.35, f32[1024]{0:T(1024)} %copy-done.7, s32[128]{0:T(128)} %dynamic_slice.34, f32[]{:T(128)} %bitcast, s32[1024]{0:T(1024)S(1)} %bitcast.26, pred[128]{0:T(512)(128)(4,1)} %dynamic_slice.33, ...), kind=kOutput, calls=%fused_computation.24 | convolution fusion | flops 404815872 | bytes 3549316 | tf_op jit(solution)/shard_map/dot_general | solution.py:123
  94.0 1.2 %copy.13 = bf16[1,128,768]{2,0,1:T(2,128)(2,1)S(1)} copy(bf16[1,128,768]{2,1,0:T(8,128)(2,1)} %fusion.11) | data formatting | bytes 393216 | tf_op jit(solution)/shard_map/reshape | solution.py:128
  95.8 1.8 %reduce = bf16[128,768]{1,0:T(8,128)(2,1)S(1)} reduce(bf16[128,1,768]{2,1,0:T(2,128)(2,1)S(1)} %bitcast.20, bf16[]{:T(256)} %broadcast.411), dimensions={1}, to_apply=%bitcast.18.reduce_sub_computation | reduce | bytes 393218
  97.6 0.7 reshape.320
  98.3 3.4 %all-to-all-start.1 = ((bf16[4,2,12288]{2,1,0:T(2,128)(2,1)}), bf16[4,2,12288]{2,1,0:T(2,128)(2,1)S(1)}, u32[]{:S(2)}, u32[]{:S(2)}) async-start(bf16[4,2,12288]{2,1,0:T(2,128)(2,1)} %reshape.320), calls=%async_computation.1 | async-start | bytes 393216 | tf_op jit(solution)/shard_map/all_to_all | solution.py:127
  101.7 1.5 %split.8 = bf16[1024,768]{1,0:T(8,128)(2,1)S(1)} slice(bf16[1024,1536]{1,0:T(8,128)(2,1)} %all-gather.2.cloned.1.call-done), slice={[0:1024], [0:768]} | slice | bytes 3145728 | tf_op jit(solution)/shard_map/split | solution.py:70
  103.3 4.2 %fusion.7 = bf16[128,768]{1,0:T(8,128)(2,1)} fusion(bf16[1024,1536]{1,0:T(8,128)(2,1)} %all-gather.2.cloned.1.call-done, f32[1024]{0:T(1024)S(1)} %copy-done.6, f32[128]{0:T(128)S(1)} %copy-done.12, s32[1024]{0:T(1024)S(1)} %fusion.58, f32[]{:T(128)} %bitcast, s32[128]{0:T(128)S(1)} %copy-done.11, pred[1024]{0:T(1024)(128)(4,1)S(1)} %copy-done.4, ...), kind=kOutput, calls=%fused_computation.22 | convolution fusion | flops 404815872 | bytes 3549704 | tf_op jit(solution)/shard_map/dot_general | solution.py:114
  109.1 1.2 %gather_fusion.2 = bf16[4,32,768]{2,1,0:T(8,128)(2,1)} fusion(bf16[4,32,768]{2,1,0:T(8,128)(2,1)S(1)} %bitcast.23, s32[1024]{0:T(1024)S(1)} %pad_clamp_fusion), kind=kCustom, calls=%fused_computation.2 | custom fusion | bytes 393232 | tf_op jit(solution)/shard_map/gather | solution.py:130
  (46 shorter events, 4.4 us)
Async XLA Ops:
  7.2 1.4 %copy-start = (bf16[4,32,768]{2,1,0:T(8,128)(2,1)S(1)}, bf16[4,32,768]{2,1,0:T(8,128)(2,1)}, u32[]{:S(2)}) copy-start(bf16[4,32,768]{2,1,0:T(8,128)(2,1)} %param.7) | copy-start | bytes 589828
  7.2 28.3 %copy-start.2 = (s32[1,1024]{1,0:T(1,128)S(1)}, s32[1,1024]{1,0:T(1,128)}, u32[]{:S(2)}) copy-start(s32[1,1024]{1,0:T(1,128)} %param.10) | copy-start | bytes 12292
  7.2 26.5 %copy-start.9 = (f32[4]{0:T(128)S(1)}, f32[4]{0:T(128)}, u32[]{:S(2)}) copy-start(f32[4]{0:T(128)} %param.11) | copy-start | bytes 52
  7.2 73.5 %all-gather.2.cloned.1.call-start = ((), (), s32[]{:S(2)}) async-start(), calls=%async_computation.2 | async-start | bytes 3538944 | tf_op jit(solution)/shard_map/all_gather | solution.py:71
  32.4 48.3 %copy-start.3 = (pred[1024]{0:T(1024)(128)(4,1)}, pred[1024]{0:T(1024)(128)(4,1)S(1)}, u32[]{:S(2)}) copy-start(pred[1024]{0:T(1024)(128)(4,1)S(1)} %broadcast_compare_fusion) | copy-start | bytes 3076
  34.9 45.9 %copy-start.8 = (pred[1024]{0:T(1024)(128)(4,1)}, pred[1024]{0:T(1024)(128)(4,1)S(1)}, u32[]{:S(2)}) copy-start(pred[1024]{0:T(1024)(128)(4,1)S(1)} %iota_compare_fusion) | copy-start | bytes 3076
  85.0 5.9 %copy-start.1 = (bf16[1024,1536]{1,0:T(8,128)(2,1)S(1)}, bf16[1024,1536]{1,0:T(8,128)(2,1)}, u32[]{:S(2)}) copy-start(bf16[1024,1536]{1,0:T(8,128)(2,1)} %all-gather.2.cloned.1.call-done) | copy-start | bytes 9437188
  89.6 0.6 copy-start.5
  89.6 0.7 copy-start.7
  94.0 9.3 %copy-start.4 = (pred[1024]{0:T(1024)(128)(4,1)S(1)}, pred[1024]{0:T(1024)(128)(4,1)}, u32[]{:S(2)}) copy-start(pred[1024]{0:T(1024)(128)(4,1)} %copy-done.3) | copy-start | bytes 3076
  94.0 9.3 %copy-start.6 = (f32[1024]{0:T(1024)S(1)}, f32[1024]{0:T(1024)}, u32[]{:S(2)}) copy-start(f32[1024]{0:T(1024)} %copy-done.5) | copy-start | bytes 12292
  94.0 9.3 %copy-start.10 = (pred[128]{0:T(512)(128)(4,1)S(1)}, pred[128]{0:T(512)(128)(4,1)}, u32[]{:S(2)}) copy-start(pred[128]{0:T(512)(128)(4,1)} %dynamic_slice.29) | copy-start | bytes 388
  94.0 9.3 %copy-start.11 = (s32[128]{0:T(128)S(1)}, s32[128]{0:T(128)}, u32[]{:S(2)}) copy-start(s32[128]{0:T(128)} %dynamic-slice_bitcast_fusion) | copy-start | bytes 1540
  94.0 9.3 %copy-start.12 = (f32[128]{0:T(128)S(1)}, f32[128]{0:T(128)}, u32[]{:S(2)}) copy-start(f32[128]{0:T(128)} %dynamic_slice.32) | copy-start | bytes 1540
  98.3 10.5 %all-to-all-start.1 = ((bf16[4,2,12288]{2,1,0:T(2,128)(2,1)}), bf16[4,2,12288]{2,1,0:T(2,128)(2,1)S(1)}, u32[]{:S(2)}, u32[]{:S(2)}) async-start(bf16[4,2,12288]{2,1,0:T(2,128)(2,1)} %reshape.320), calls=%async_computation.1 | async-start | bytes 393216 | tf_op jit(solution)/shard_map/all_to_all | solution.py:127
Sparse Core Ops, SparseCore 0:
  20.3 60.3 all-gather.1
